TPU v7x, 128 devices: a whole 4x4x4 slice. The times are simulated.
128 devices in a mesh: req: 8 (over x, core), seq: 16 (over z, y).
Axes of the slice: x: 4, y: 4, z: 4, core: 2. Of those that a mesh axis runs over, the one named last changes fastest.
Arguments:
- hidden: bfloat16 [8, 2048, 2048], P('req', 'seq'), may hold values from -6 to 6
- lengths: int32 [8], replicated, may hold values from 1 to 2048, 10240 in all
- slot_request: int32 [8], replicated, may hold values from 0 to 7, each once
- norm_gain: bfloat16 [2048], replicated, may hold values from 0.099609375 to 1.8984375
- in_weight: bfloat16 [2, 2048, 4096], P(None, 'req', 'seq'), may hold values from -0.125 to 0.125
- conv_weight: bfloat16 [4, 4096], P(None, 'seq'), may hold values from -3 to 3
- conv_bias: bfloat16 [4096], P('seq'), may hold values from -0.5 to 0.5
- xproj_weight: bfloat16 [4096, 160], P('seq'), may hold values from -0.09375 to 0.09375
- dt_weight: bfloat16 [128, 4096], P(None, 'seq'), may hold values from -0.5 to 0.5
- dt_bias: bfloat16 [4096], P('seq'), may hold values from -6.91 to -2.25
- a_log: float32 [16, 4096], replicated, may hold values from -2.3 to 1.39
- skip_gain: float32 [4096], replicated, may hold values from 0.5 to 1.5
- out_weight: bfloat16 [4096, 2048], P('seq', 'req'), may hold values from -0.09375 to 0.09375
Outputs:
- mixed: bfloat16 [8, 2048, 2048], P('req', 'seq')
- final_state: float32 [8, 16, 4096], P('req', None, 'seq')
Inputs may be any that keep to these rules, and one draw needn't show every extreme that they name: `lengths`: each slot's length is at least 1, the longest is exactly 2048, and they sum to 10240. `slot_request`: A permutation of the requests.
All inputs are finite; a program needn't handle non-finite values.
Results may differ from a plain program's by a relative error of at most 0.015.
Values may be sent and summed in bfloat16 or wider, within the bound.
No kernel may reach another device: no remote copies, remote signals or barrier semaphores. Data moves between devices by JAX's collectives and lax.ppermute only.
A program may use at most 128 MiB of HBM per device.

v0:
```python
import jax
import jax.numpy as jnp
from jax import lax
from jax.sharding import PartitionSpec as P

STATE = 16
RANK = 128


def shifted(block, axis, distance):
    devices = range(lax.axis_size(axis))
    route = [(i - distance, i) for i in devices if i - distance in devices]
    return lax.ppermute(block, axis, route)


def spread(array, axis, root):
    mine = lax.axis_index(axis) == root
    return lax.psum(jnp.where(mine, array, jnp.zeros_like(array)), axis)


def to_blocks(array):
    pieces, length, columns = array.shape
    return jnp.moveaxis(array.reshape(pieces, 16, length // 16, columns), 1, 0)


def from_blocks(array):
    count, pieces, group, columns = array.shape
    return jnp.moveaxis(array, 0, 1).reshape(pieces, count * group, columns)


def piece_scan(rates, values, entry, readout, decay):
    pieces, length, columns = rates.shape
    group = length // 16
    positions = jnp.arange(length, dtype=jnp.int32)
    lower = (positions[None, :] <= positions[:, None]).astype(jnp.float32)
    running = jnp.einsum("rs,psw->prw", lower, rates, precision=lax.Precision.HIGHEST)

    def advance(state, items):
        rate, value, into, outof = items
        outputs = []
        for place in range(group):
            factor = jnp.exp(rate[:, place][:, None, :] * decay[None])
            state = (
                factor * state
                + (rate[:, place] * value[:, place])[:, None, :] * into[:, place][:, :, None]
            )
            outputs.append(jnp.sum(outof[:, place][:, :, None] * state, axis=1))
        return (state, jnp.stack(outputs, axis=1))

    start = jnp.zeros((pieces, decay.shape[0], columns), jnp.float32)
    end_local, local_out = lax.scan(
        advance, start, (to_blocks(rates), to_blocks(values), to_blocks(entry), to_blocks(readout))
    )
    total_decay = jnp.exp(running[:, length - 1][:, None, :] * decay[None])
    return (end_local, from_blocks(local_out), total_decay, running)


def carried_part(running, readout, decay, carry_in):

    def correct(items):
        total, outof = items
        kept = jnp.exp(total[:, :, None, :] * decay[None, None]) * carry_in[:, None]
        return jnp.sum(outof[:, :, :, None] * kept, axis=2)

    return from_blocks(lax.map(correct, (to_blocks(running), to_blocks(readout))))


def per_device(
    hidden,
    lengths,
    slot_request,
    norm_gain,
    in_weight,
    conv_weight,
    conv_bias,
    xproj_weight,
    dt_weight,
    dt_bias,
    a_log,
    skip_gain,
    out_weight,
):
    seq_count = lax.axis_size("seq")
    seq_index = lax.axis_index("seq")
    req_index = lax.axis_index("req")
    rows = hidden.shape[1]
    span = rows * seq_count
    width = in_weight.shape[2]
    taps_count = conv_weight.shape[0]
    state_count = a_log.shape[0]
    total_inner = a_log.shape[1]
    tokens = hidden[0].astype(jnp.float32)
    scale = lax.rsqrt(jnp.mean(tokens * tokens, axis=-1, keepdims=True) + 1e-05)
    normed = (tokens * scale * norm_gain.astype(jnp.float32)).astype(jnp.bfloat16)
    w_in = lax.all_gather(in_weight, "req", axis=1, tiled=True)
    w_flat = jnp.concatenate((w_in[0], w_in[1]), axis=1)
    both = jnp.dot(
        lax.all_gather(normed, "seq", axis=0, tiled=True),
        w_flat,
        preferred_element_type=jnp.float32,
    )
    xin = both[:, :width]
    zgate = both[:, width:].astype(jnp.bfloat16)
    padded = jnp.pad(xin, ((taps_count - 1, 0), (0, 0)))
    taps = conv_weight.astype(jnp.float32)
    convolved = conv_bias.astype(jnp.float32) + jnp.zeros_like(xin)
    for tap in range(taps_count):
        convolved = convolved + taps[tap] * padded[tap : tap + span, :]
    inner = jax.nn.silu(convolved).astype(jnp.bfloat16)
    partial_proj = jnp.dot(inner, xproj_weight, preferred_element_type=jnp.float32)
    length_here = lax.dynamic_index_in_dim(lengths, req_index, 0, keepdims=False)
    summed = lax.psum(partial_proj, "seq")
    live_all = (jnp.arange(span, dtype=jnp.int32) < length_here).astype(jnp.float32)
    rate_low = summed[:, :RANK].astype(jnp.bfloat16)
    delta_ch = (
        jax.nn.softplus(
            jnp.dot(rate_low, dt_weight, preferred_element_type=jnp.float32)
            + dt_bias.astype(jnp.float32)
        )
        * live_all[:, None]
    )
    w_out = lax.all_gather(out_weight, "req", axis=1, tiled=True)
    inner_tok = lax.all_to_all(inner, "seq", split_axis=0, concat_axis=1, tiled=True)
    delta_tok = lax.all_to_all(
        delta_ch.astype(jnp.bfloat16), "seq", split_axis=0, concat_axis=1, tiled=True
    ).astype(delta_ch.dtype)
    own_proj = lax.dynamic_slice_in_dim(summed, seq_index * rows, rows, 0)
    decay = -jnp.exp(a_log)
    inner_f = inner_tok.astype(jnp.float32)
    entry = own_proj[None, :, RANK : RANK + STATE]
    readout = own_proj[None, :, RANK + STATE :]
    end_local, local_out, total_decay, running = piece_scan(
        delta_tok[None], inner_f[None], entry, readout, decay
    )
    zeros_state = jnp.zeros((state_count, total_inner), jnp.float32)

    def relay(turn, incoming):
        return shifted(total_decay[0] * incoming + end_local[0], "seq", 1)

    carry_in = lax.fori_loop(0, seq_count - 1, relay, zeros_state)
    carried = carried_part(running, readout, decay, carry_in[None])
    scanned = ((local_out + carried)[0] + skip_gain * inner_f).astype(jnp.bfloat16)
    last = spread(
        (total_decay[0] * carry_in + end_local[0]).astype(jnp.bfloat16), "seq", seq_count - 1
    ).astype(jnp.float32)
    mine = lax.dynamic_slice_in_dim(last, seq_index * width, width, 1)
    scanned_ch = lax.all_to_all(scanned, "seq", split_axis=1, concat_axis=0, tiled=True)
    gated_ch = (scanned_ch.astype(jnp.float32) * jax.nn.silu(zgate.astype(jnp.float32))).astype(
        jnp.bfloat16
    )
    branch = lax.psum_scatter(
        jnp.dot(gated_ch, w_out, preferred_element_type=jnp.float32).astype(jnp.bfloat16),
        "seq",
        scatter_dimension=0,
        tiled=True,
    ).astype(jnp.float32)
    slot_all = lax.all_gather(mine[None], "req", axis=0, tiled=True)
    picked = (slot_request == req_index).astype(jnp.float32)
    final_state = jnp.sum(picked[:, None, None] * slot_all, axis=0, keepdims=True)
    mixed = (tokens + branch).astype(jnp.bfloat16)[None]
    return (mixed, final_state)


def solution(mesh):
    in_specs = (
        P("req", "seq", None),
        P(),
        P(),
        P(),
        P(None, "req", "seq"),
        P(None, "seq"),
        P("seq"),
        P("seq", None),
        P(None, "seq"),
        P("seq"),
        P(),
        P(),
        P("seq", "req"),
    )
    out_specs = (P("req", "seq", None), P("req", None, "seq"))
    return jax.shard_map(
        per_device, mesh=mesh, in_specs=in_specs, out_specs=out_specs, check_vma=False
    )
```

profile of v0, /device:TPU:0, one launch (start us, length us, event | category | flops | bytes accessed | tf_op | source)
XLA Modules:
  0.0 717.7 jit_solution(14593859675135900258)
XLA Ops:
  9.9 2.0 fusion.42
  12.1 25.4 %all-gather.7.cloned.1.call-done = bf16[2,2048,256]{2,1,0:T(8,128)(2,1)} async-done(((bf16[2,256,256]{2,1,0:T(8,128)(2,1)}), bf16[2,2048,256]{2,1,0:T(8,128)(2,1)}) %all-gather.7.cloned.1.call-update) | async-done | bytes 2097168 | tf_op jit(solution)/shard_map/all_gather | solution.py:95
  37.5 1.7 slice_bitcast_fusion.17
  39.2 72.3 %all-gather.5.cloned.1.call-done = bf16[2048,2048]{1,0:T(8,128)(2,1)} async-done(((bf16[128,2048]{1,0:T(8,128)(2,1)}), bf16[2048,2048]{1,0:T(8,128)(2,1)}) %all-gather.5.cloned.1.call-update) | async-done | bytes 8388624 | tf_op jit(solution)/shard_map/all_gather | solution.py:98
  111.5 6.9 fusion.33
  118.6 1.7 copy-done.4
  120.3 2.3 multiply_convert_fusion
  122.7 2.8 fusion.56
  125.5 5.4 all-to-all-start.1
  132.2 88.7 %all-reduce.4.cloned.1.call-done = f32[2048,160]{0,1:T(8,128)} async-done(((f32[2048,160]{0,1:T(8,128)}), f32[2048,160]{0,1:T(8,128)}) %all-reduce.4.cloned.1.call-update) | async-done | bytes 1310736 | tf_op jit(solution)/shard_map/psum | solution.py:112
  220.9 2.7 fusion.32
  223.6 1.3 copy.43
  225.0 5.1 all-to-all-start
  231.5 2.6 copy.45
  234.1 2.8 reshape.994
  238.4 7.5 %all-to-all-done = bf16[16,128,256]{1,2,0:T(8,128)(2,1)S(1)} async-done(((bf16[16,128,256]{1,2,0:T(8,128)(2,1)}), bf16[16,128,256]{1,2,0:T(8,128)(2,1)S(1)}, u32[]{:S(2)}, u32[]{:S(2)}) %all-to-all-start) | async-done | bytes 1048608 | tf_op jit(solution)/shard_map/all_to_all | solution.py:124
  247.7 1.6 bitcast_convert_fusion
  249.3 2.2 copy.44
  251.6 1.6 reshape.993
  254.2 1.5 broadcast.550.clone
  255.7 65.7 %while.35 = (s32[]{:T(128)}, f32[1,16,4096]{2,1,0:T(8,128)S(1)}, f32[16,1,8,4096]{3,2,1,0:T(8,128)}, f32[16,1,8,4096]{3,2,1,0:T(8,128)}, f32[16,4096]{1,0:T(8,12...) while((s32[]{:T(128)}, f32[1,16,4096]{2,1,0:T(8,128)S(1)}, ...), condition=%wide.region_11.12_spmd.clone, body=%wide.region_2.11_spmd.clone.sunk | while | flops 4849667 | bytes 4347896 | solution.py:51
  321.5 148.6 %while.33 = (s32[]{:T(128)}, f32[16,4096]{1,0:T(8,128)S(1)}, f32[1,16,4096]{2,1,0:T(8,128)S(1)}, f32[1,16,4096]{2,1,0:T(8,128)S(1)}, s32[]{:T(128)}) while((s32[]{:T(128)}, f32[16,4096]{1,0:T(8,128)S(1)}, f32[1,16,4096]{2,1,0:T(8,128)S(1)}, f32[1,16,4096]{2,1,0:T(8,128)S(1)}, s32[]{:T(128)}) %tuple.124), condition=%wide.region_13.14_spmd, body=%wide.region_12.13_spmd.sunk | while | flops 131074 | bytes 2097253 | solution.py:140
  321.5 2.5 collective-permute-start
  324.1 3.9 collective-permute-done
  328.0 4.4 collective-permute-start
  332.4 5.0 collective-permute-done
  337.4 4.4 collective-permute-start
  341.8 6.1 collective-permute-done
  347.9 4.4 collective-permute-start
  352.4 6.1 collective-permute-done
  358.5 4.4 collective-permute-start
  362.9 5.2 collective-permute-done
  368.1 4.4 collective-permute-start
  372.5 4.3 collective-permute-done
  376.9 4.4 collective-permute-start
  381.3 3.9 collective-permute-done
  385.2 6.8 collective-permute-start
  392.1 5.6 collective-permute-done
  397.7 6.2 collective-permute-start
  404.0 4.5 collective-permute-done
  408.5 5.6 collective-permute-start
  414.1 3.9 collective-permute-done
  418.0 6.5 collective-permute-start
  424.5 3.9 collective-permute-done
  428.4 6.5 collective-permute-start
  435.0 3.9 collective-permute-done
  438.9 6.5 collective-permute-start
  445.4 3.9 collective-permute-done
  449.3 6.5 collective-permute-start
  455.8 3.9 collective-permute-done
  459.7 6.5 collective-permute-start
  466.2 3.9 collective-permute-done
  470.1 1.6 broadcast.550
  471.6 35.8 %while.34 = (s32[]{:T(128)}, f32[16,1,8,4096]{3,2,1,0:T(8,128)}, f32[16,1,8,16]{3,2,1,0:T(8,128)S(1)}, f32[16,1,8,4096]{3,2,1,0:T(8,128)}, f32[16,4096]{1,0:T(8,128)S(1)}, /*index=5*/f32[16,4096]{1,0:T(8,128)S(1)}, s32[]{:T(128)}) while((s32[]{:T(128)}, f32[16,1,8,4096]{3,2,1,0:T(8,128)}, f32[16,1,8,16]{3,2,1,0:T(8,128)S(1)}, ...), condition=%wide.region_16.17_spmd, body=%wide.region_14.16_spmd.sunk | while | flops 2064386 | bytes 1312853 | solution.py:65
  507.4 2.5 add.134
  510.6 2.3 fusion.30
  512.9 18.0 %all-to-all-start.2 = ((bf16[128,16,256]{2,0,1:T(8,128)(2,1)}), bf16[128,16,256]{2,0,1:T(8,128)(2,1)S(1)}, u32[]{:S(2)}, u32[]{:S(2)}) async-start(bf16[128,16,256]{2,0,1:T(8,128)(2,1)} %fusion.30), calls=%async_computation.2 | async-start | bytes 2097152 | tf_op jit(solution)/shard_map/all_to_all | solution.py:147
  532.1 12.2 %all-to-all-done.2 = bf16[128,16,256]{2,0,1:T(8,128)(2,1)S(1)} async-done(((bf16[128,16,256]{2,0,1:T(8,128)(2,1)}), bf16[128,16,256]{2,0,1:T(8,128)(2,1)S(1)}, u32[]{:S(2)}, u32[]{:S(2)}) %all-to-all-start.2) | async-done | bytes 1048608 | tf_op jit(solution)/shard_map/all_to_all | solution.py:147
  544.3 2.3 fusion.39
  546.7 6.8 convolution_convert_fusion
  554.1 66.1 %all-reduce.6.cloned.1.call-done = bf16[16,4096]{1,0:T(8,128)(2,1)} async-done(((bf16[16,4096]{1,0:T(8,128)(2,1)}), bf16[16,4096]{1,0:T(8,128)(2,1)}) %all-reduce.6.cloned.1.call-update) | async-done | bytes 131088 | tf_op jit(solution)/shard_map/psum | solution.py:18
  620.9 13.0 %all-gather = f32[128,256]{1,0:T(8,128)S(1)} all-gather(f32[16,256]{1,0:T(8,128)S(1)} %dynamic-slice_convert_fusion), channel_id=2, replica_groups=mesh['req'=8,'seq'=16] {'req'}, dimensions={0}, use_global_device_ids=true | all-gather | bytes 147456 | tf_op jit(solution)/shard_map/all_gather | solution.py:157
  634.6 74.3 %reduce-scatter.2.cloned.1.call-done = bf16[128,2048]{1,0:T(8,128)(2,1)} async-done(((bf16[2048,2048]{1,0:T(8,128)(2,1)}), bf16[128,2048]{1,0:T(8,128)(2,1)}) %reduce-scatter.2.cloned.1.call-update) | async-done | bytes 524304 | tf_op jit(solution)/shard_map/reduce_scatter | solution.py:151
  708.9 2.0 fusion.44
  (324 shorter events, 114.9 us)
Async XLA Ops:
  7.2 115.5 %copy-start = (bf16[256,160]{0,1:T(8,128)(2,1)S(1)}, bf16[256,160]{0,1:T(8,128)(2,1)}, u32[]{:S(2)}) copy-start(bf16[256,160]{0,1:T(8,128)(2,1)} %param.26) | copy-start | bytes 245764
  7.2 4.8 copy-start.12
  7.2 4.8 copy-start.10
  7.2 30.3 %all-gather.7.cloned.1.call-start = ((), (), s32[]{:S(2)}) async-start(), calls=%async_computation.5 | async-start | bytes 2359296 | tf_op jit(solution)/shard_map/all_gather | solution.py:95
  7.9 103.6 %all-gather.5.cloned.1.call-start = ((), (), s32[]{:S(2)}) async-start(), calls=%async_computation.4 | async-start | bytes 8912896 | tf_op jit(solution)/shard_map/all_gather | solution.py:98
  12.0 209.0 %all-reduce.4.cloned.1.call-start = ((), (), s32[]{:S(2)}) async-start(), calls=%async_computation.6 | async-start | bytes 2621440 | tf_op jit(solution)/shard_map/psum | solution.py:112
  118.4 2.0 copy-start.4
  125.5 5.5 copy-start.13
  125.5 5.5 copy-start.14
  125.5 95.4 %copy-start.11 = (bf16[128,256]{1,0:T(8,128)(2,1)S(1)}, bf16[128,256]{1,0:T(8,128)(2,1)}, u32[]{:S(2)}) copy-start(bf16[128,256]{1,0:T(8,128)(2,1)} %param.27) | copy-start | bytes 196612
  125.5 99.5 %all-to-all-start.1 = ((bf16[16,128,256]{2,1,0:T(8,128)(2,1)}), bf16[16,128,256]{2,1,0:T(8,128)(2,1)S(1)}, u32[]{:S(2)}, u32[]{:S(2)}) async-start(bf16[16,128,256]{2,1,0:T(8,128)(2,1)} %bitcast.17), calls=%async_computation.1 | async-start | bytes 2097152 | tf_op jit(solution)/shard_map/all_to_all | solution.py:123
  223.6 7.1 copy-start.9
  225.0 20.9 %all-to-all-start = ((bf16[16,128,256]{1,2,0:T(8,128)(2,1)}), bf16[16,128,256]{1,2,0:T(8,128)(2,1)S(1)}, u32[]{:S(2)}, u32[]{:S(2)}) async-start(bf16[16,128,256]{1,2,0:T(8,128)(2,1)} %copy.43), calls=%async_computation | async-start | bytes 2097152 | tf_op jit(solution)/shard_map/all_to_all | solution.py:124
  230.1 316.6 %all-gather.9.cloned.1.call-start = ((), (), s32[]{:S(2)}) async-start(), calls=%async_computation.7 | async-start | bytes 1179648 | tf_op jit(solution)/shard_map/all_gather | solution.py:122
  246.3 1.3 copy-start.3
  247.7 5.4 copy-start.6
  321.5 6.4 collective-permute-start
  328.0 9.4 %collective-permute-start = (f32[16,4096]{1,0:T(8,128)S(1)}, f32[16,4096]{1,0:T(8,128)S(1)}, u32[]{:S(2)}, u32[]{:S(2)}) collective-permute-start(f32[16,4096]{1,0:T(8,128)S(1)} %bitcast_add_fusion.3), channel_id=1, source_target_pairs={{0,1},{1,2},{2,3},{3,4},{4,5},{5,6},{6,7},{7,8},{8,9},{9,10},{10,1... | collective-permute-start | bytes 786440 | tf_op jit(solution)/shard_map/while/body/eval_jaxpr/ppermute | solution.py:13
  337.4 10.5 %collective-permute-start = (f32[16,4096]{1,0:T(8,128)S(1)}, f32[16,4096]{1,0:T(8,128)S(1)}, u32[]{:S(2)}, u32[]{:S(2)}) collective-permute-start(f32[16,4096]{1,0:T(8,128)S(1)} %bitcast_add_fusion.3), channel_id=1, source_target_pairs={{0,1},{1,2},{2,3},{3,4},{4,5},{5,6},{6,7},{7,8},{8,9},{9,10},{10,1... | collective-permute-start | bytes 786440 | tf_op jit(solution)/shard_map/while/body/eval_jaxpr/ppermute | solution.py:13
  347.9 10.5 %collective-permute-start = (f32[16,4096]{1,0:T(8,128)S(1)}, f32[16,4096]{1,0:T(8,128)S(1)}, u32[]{:S(2)}, u32[]{:S(2)}) collective-permute-start(f32[16,4096]{1,0:T(8,128)S(1)} %bitcast_add_fusion.3), channel_id=1, source_target_pairs={{0,1},{1,2},{2,3},{3,4},{4,5},{5,6},{6,7},{7,8},{8,9},{9,10},{10,1... | collective-permute-start | bytes 786440 | tf_op jit(solution)/shard_map/while/body/eval_jaxpr/ppermute | solution.py:13
  358.5 9.6 %collective-permute-start = (f32[16,4096]{1,0:T(8,128)S(1)}, f32[16,4096]{1,0:T(8,128)S(1)}, u32[]{:S(2)}, u32[]{:S(2)}) collective-permute-start(f32[16,4096]{1,0:T(8,128)S(1)} %bitcast_add_fusion.3), channel_id=1, source_target_pairs={{0,1},{1,2},{2,3},{3,4},{4,5},{5,6},{6,7},{7,8},{8,9},{9,10},{10,1... | collective-permute-start | bytes 786440 | tf_op jit(solution)/shard_map/while/body/eval_jaxpr/ppermute | solution.py:13
  368.1 8.8 %collective-permute-start = (f32[16,4096]{1,0:T(8,128)S(1)}, f32[16,4096]{1,0:T(8,128)S(1)}, u32[]{:S(2)}, u32[]{:S(2)}) collective-permute-start(f32[16,4096]{1,0:T(8,128)S(1)} %bitcast_add_fusion.3), channel_id=1, source_target_pairs={{0,1},{1,2},{2,3},{3,4},{4,5},{5,6},{6,7},{7,8},{8,9},{9,10},{10,1... | collective-permute-start | bytes 786440 | tf_op jit(solution)/shard_map/while/body/eval_jaxpr/ppermute | solution.py:13
  376.9 8.3 %collective-permute-start = (f32[16,4096]{1,0:T(8,128)S(1)}, f32[16,4096]{1,0:T(8,128)S(1)}, u32[]{:S(2)}, u32[]{:S(2)}) collective-permute-start(f32[16,4096]{1,0:T(8,128)S(1)} %bitcast_add_fusion.3), channel_id=1, source_target_pairs={{0,1},{1,2},{2,3},{3,4},{4,5},{5,6},{6,7},{7,8},{8,9},{9,10},{10,1... | collective-permute-start | bytes 786440 | tf_op jit(solution)/shard_map/while/body/eval_jaxpr/ppermute | solution.py:13
  385.2 12.5 %collective-permute-start = (f32[16,4096]{1,0:T(8,128)S(1)}, f32[16,4096]{1,0:T(8,128)S(1)}, u32[]{:S(2)}, u32[]{:S(2)}) collective-permute-start(f32[16,4096]{1,0:T(8,128)S(1)} %bitcast_add_fusion.3), channel_id=1, source_target_pairs={{0,1},{1,2},{2,3},{3,4},{4,5},{5,6},{6,7},{7,8},{8,9},{9,10},{10,1... | collective-permute-start | bytes 786440 | tf_op jit(solution)/shard_map/while/body/eval_jaxpr/ppermute | solution.py:13
  397.7 10.7 %collective-permute-start = (f32[16,4096]{1,0:T(8,128)S(1)}, f32[16,4096]{1,0:T(8,128)S(1)}, u32[]{:S(2)}, u32[]{:S(2)}) collective-permute-start(f32[16,4096]{1,0:T(8,128)S(1)} %bitcast_add_fusion.3), channel_id=1, source_target_pairs={{0,1},{1,2},{2,3},{3,4},{4,5},{5,6},{6,7},{7,8},{8,9},{9,10},{10,1... | collective-permute-start | bytes 786440 | tf_op jit(solution)/shard_map/while/body/eval_jaxpr/ppermute | solution.py:13
  408.5 9.5 %collective-permute-start = (f32[16,4096]{1,0:T(8,128)S(1)}, f32[16,4096]{1,0:T(8,128)S(1)}, u32[]{:S(2)}, u32[]{:S(2)}) collective-permute-start(f32[16,4096]{1,0:T(8,128)S(1)} %bitcast_add_fusion.3), channel_id=1, source_target_pairs={{0,1},{1,2},{2,3},{3,4},{4,5},{5,6},{6,7},{7,8},{8,9},{9,10},{10,1... | collective-permute-start | bytes 786440 | tf_op jit(solution)/shard_map/while/body/eval_jaxpr/ppermute | solution.py:13
  418.0 10.4 %collective-permute-start = (f32[16,4096]{1,0:T(8,128)S(1)}, f32[16,4096]{1,0:T(8,128)S(1)}, u32[]{:S(2)}, u32[]{:S(2)}) collective-permute-start(f32[16,4096]{1,0:T(8,128)S(1)} %bitcast_add_fusion.3), channel_id=1, source_target_pairs={{0,1},{1,2},{2,3},{3,4},{4,5},{5,6},{6,7},{7,8},{8,9},{9,10},{10,1... | collective-permute-start | bytes 786440 | tf_op jit(solution)/shard_map/while/body/eval_jaxpr/ppermute | solution.py:13
  428.4 10.4 %collective-permute-start = (f32[16,4096]{1,0:T(8,128)S(1)}, f32[16,4096]{1,0:T(8,128)S(1)}, u32[]{:S(2)}, u32[]{:S(2)}) collective-permute-start(f32[16,4096]{1,0:T(8,128)S(1)} %bitcast_add_fusion.3), channel_id=1, source_target_pairs={{0,1},{1,2},{2,3},{3,4},{4,5},{5,6},{6,7},{7,8},{8,9},{9,10},{10,1... | collective-permute-start | bytes 786440 | tf_op jit(solution)/shard_map/while/body/eval_jaxpr/ppermute | solution.py:13
  438.9 10.4 %collective-permute-start = (f32[16,4096]{1,0:T(8,128)S(1)}, f32[16,4096]{1,0:T(8,128)S(1)}, u32[]{:S(2)}, u32[]{:S(2)}) collective-permute-start(f32[16,4096]{1,0:T(8,128)S(1)} %bitcast_add_fusion.3), channel_id=1, source_target_pairs={{0,1},{1,2},{2,3},{3,4},{4,5},{5,6},{6,7},{7,8},{8,9},{9,10},{10,1... | collective-permute-start | bytes 786440 | tf_op jit(solution)/shard_map/while/body/eval_jaxpr/ppermute | solution.py:13
  449.3 10.4 %collective-permute-start = (f32[16,4096]{1,0:T(8,128)S(1)}, f32[16,4096]{1,0:T(8,128)S(1)}, u32[]{:S(2)}, u32[]{:S(2)}) collective-permute-start(f32[16,4096]{1,0:T(8,128)S(1)} %bitcast_add_fusion.3), channel_id=1, source_target_pairs={{0,1},{1,2},{2,3},{3,4},{4,5},{5,6},{6,7},{7,8},{8,9},{9,10},{10,1... | collective-permute-start | bytes 786440 | tf_op jit(solution)/shard_map/while/body/eval_jaxpr/ppermute | solution.py:13
  459.7 10.4 %collective-permute-start = (f32[16,4096]{1,0:T(8,128)S(1)}, f32[16,4096]{1,0:T(8,128)S(1)}, u32[]{:S(2)}, u32[]{:S(2)}) collective-permute-start(f32[16,4096]{1,0:T(8,128)S(1)} %bitcast_add_fusion.3), channel_id=1, source_target_pairs={{0,1},{1,2},{2,3},{3,4},{4,5},{5,6},{6,7},{7,8},{8,9},{9,10},{10,1... | collective-permute-start | bytes 786440 | tf_op jit(solution)/shard_map/while/body/eval_jaxpr/ppermute | solution.py:13
  509.9 0.7 copy-start.8
  512.9 18.1 %copy-start.5 = (f32[16,4096]{1,0:T(8,128)S(1)}, f32[16,4096]{1,0:T(8,128)}, u32[]{:S(2)}) copy-start(f32[16,4096]{1,0:T(8,128)} %param.29) | copy-start | bytes 786436
  512.9 18.1 %copy-start.7 = (f32[1,1,4096]{2,1,0:T(1,128)S(1)}, f32[1,1,4096]{2,1,0:T(1,128)}, u32[]{:S(2)}) copy-start(f32[1,1,4096]{2,1,0:T(1,128)} %copy-done.6) | copy-start | bytes 49156
  512.9 31.4 %all-to-all-start.2 = ((bf16[128,16,256]{2,0,1:T(8,128)(2,1)}), bf16[128,16,256]{2,0,1:T(8,128)(2,1)S(1)}, u32[]{:S(2)}, u32[]{:S(2)}) async-start(bf16[128,16,256]{2,0,1:T(8,128)(2,1)} %fusion.30), calls=%async_computation.2 | async-start | bytes 2097152 | tf_op jit(solution)/shard_map/all_to_all | solution.py:147
  531.0 89.2 %all-reduce.6.cloned.1.call-start = ((), (), s32[]{:S(2)}) async-start(), calls=%async_computation.9 | async-start | bytes 262144 | tf_op jit(solution)/shard_map/psum | solution.py:18
  531.8 177.1 %reduce-scatter.2.cloned.1.call-start = ((), (), s32[]{:S(2)}) async-start(), calls=%async_computation.8 | async-start | bytes 8912896 | tf_op jit(solution)/shard_map/reduce_scatter | solution.py:151
  553.5 0.7 copy-start.15
  553.5 155.5 %copy-start.2 = (bf16[1,128,2048]{2,1,0:T(8,128)(2,1)S(1)}, bf16[1,128,2048]{2,1,0:T(8,128)(2,1)}, u32[]{:S(2)}) copy-start(bf16[1,128,2048]{2,1,0:T(8,128)(2,1)} %param.19) | copy-start | bytes 1572868
  553.5 157.4 %copy-start.1 = (bf16[256,160]{0,1:T(8,128)(2,1)S(1)}, bf16[256,160]{0,1:T(8,128)(2,1)}, u32[]{:S(2)}) copy-start(bf16[256,160]{0,1:T(8,128)(2,1)} %param.26) | copy-start | bytes 245764
Sparse Core Ops, SparseCore 0:
  9.7 27.7 all-gather.6
  40.2 71.2 all-gather.4
  125.6 95.2 all-reduce.3
  232.3 24.7 all-gather.8
  535.2 84.9 all-reduce.5
  623.5 85.3 reduce-scatter.1
where the time goes:
time: 720 us; the launch traced here: 718 us
  waiting for transfers between devices  415 us (58%)
  starting transfers between devices  109 us (15%)
  local copies, waits for them, and re-layouts  89.9 us (12%)
  other arithmetic  54.7 us (8%)
  matrix products  19.6 us (3%)
  between operations  14.4 us (2%)
  blocking collectives  13 us (2%)
    psum x1, waiting for transfers between devices, per_device(): summed = lax.psum(partial_proj, 'seq')  88.7 us
    ppermute x15, starting transfers between devices, shifted(): return lax.ppermute(block, axis, route)  80.1 us
    reduce_scatter x1, waiting for transfers between devices, per_device(): lax.psum_scatter(jnp.dot(gated_ch, w_out, preferred_element_type=jnp.floa...  74.3 us
    all_gather x1, waiting for transfers between devices, per_device(): lax.all_gather(normed, 'seq', axis=0, tiled=True)  72.3 us
    ppermute x15, waiting for transfers between devices, shifted(): return lax.ppermute(block, axis, route)  67.6 us
    psum x1, waiting for transfers between devices, spread(): return lax.psum(jnp.where(mine, array, jnp.zeros_like(array)), axis)  66.1 us
    squeeze x32, local copies, waits for them, and re-layouts, piece_scan(): lax.scan(advance, start, (to_blocks(rates), to_blocks(values), to_blocks(...  26.9 us
    all_gather x1, waiting for transfers between devices, per_device(): w_in = lax.all_gather(in_weight, 'req', axis=1, tiled=True)  25.4 us
  transfers between devices with their start and end apart: 24, of which 22 were waited for; matrix products, arithmetic and copies ran while one was open for 20% of the time, Pallas kernels for 0%

commit v1 on v0

--- a/solution.py
+++ b/solution.py
@@ -5,6 +5,12 @@
 
 STATE = 16
 RANK = 128
+
+
+def joined_along(blocks, dim):
+    blocks = jnp.moveaxis(blocks, 0, dim)
+    shape = blocks.shape
+    return blocks.reshape(*shape[:dim], shape[dim] * shape[dim + 1], *shape[dim + 2 :])
 
 
 def shifted(block, axis, distance):
@@ -92,7 +98,19 @@
     tokens = hidden[0].astype(jnp.float32)
     scale = lax.rsqrt(jnp.mean(tokens * tokens, axis=-1, keepdims=True) + 1e-05)
     normed = (tokens * scale * norm_gain.astype(jnp.float32)).astype(jnp.bfloat16)
-    w_in = lax.all_gather(in_weight, "req", axis=1, tiled=True)
+    size = lax.axis_size("req")
+    pairs = [(i_2, (i_2 + 1) % size) for i_2 in range(size)]
+    back = [(b, a) for a, b in pairs]
+    lower_2, upper = ([], [])
+    for lap in range(size - 1):
+        if lap % 2 == 0:
+            lower_2.append(lax.ppermute(lower_2[-1] if lower_2 else in_weight, "req", pairs))
+        else:
+            upper.append(lax.ppermute(upper[-1] if upper else in_weight, "req", back))
+    pieces_2 = jnp.stack([*lower_2[::-1], in_weight, *upper])
+    shift = lax.axis_index("req") - len(lower_2)
+    pieces_2 = pieces_2[(jnp.arange(size) - shift) % size]
+    w_in = joined_along(pieces_2, 1)
     w_flat = jnp.concatenate((w_in[0], w_in[1]), axis=1)
     both = jnp.dot(
         lax.all_gather(normed, "seq", axis=0, tiled=True),

time: 720 us -> 696 us (0.967)
  waiting for transfers between devices: 415 us -> 372 us
  starting transfers between devices: 109 us -> 118 us
  local copies, waits for them, and re-layouts: 89.9 us -> 97.8 us
    all_gather x1, waiting for transfers between devices: 72.3 us -> 36.2 us  [per_device(): lax.all_gather(normed, 'seq', axis=0, tiled=True)]
    all_gather x1 -> x0, waiting for transfers between devices: 25.4 us -> none  [per_device(): w_in = lax.all_gather(in_weight, 'req', axis=1, tiled=True)]
    ppermute x0 -> x7, waiting for transfers between devices: none -> 19.1 us  [the longest x4 19 us: per_device(): lax.ppermute(lower_2[-1] if lower_2 else in_weight, 'req', pairs)]
    ppermute x0 -> x7, starting transfers between devices: none -> 8.9 us  [the longest x3 8.87 us: per_device(): upper.append(lax.ppermute(upper[-1] if upper else in_weight, 'req', back))]
  transfers between devices with their start and end apart: 24 -> 30, of which waited for: 22 -> 25; matrix products, arithmetic and copies ran while one was open for 20% -> 22% of each run, Pallas kernels for 0% -> 0%
where the time goes in v1:
time: 696 us; the launch traced here: 693 us
  waiting for transfers between devices  372 us (53%)
  starting transfers between devices  118 us (17%)
  local copies, waits for them, and re-layouts  97.8 us (14%)
  other arithmetic  54.8 us (8%)
  matrix products  20 us (3%)
  between operations  15.6 us (2%)
  blocking collectives  13 us (2%)
    psum x1, waiting for transfers between devices, per_device(): summed = lax.psum(partial_proj, 'seq')  88.7 us
    ppermute x15, starting transfers between devices, shifted(): return lax.ppermute(block, axis, route)  80.2 us
    reduce_scatter x1, waiting for transfers between devices, per_device(): lax.psum_scatter(jnp.dot(gated_ch, w_out, preferred_element_type=jnp.floa...  74.3 us
    ppermute x15, waiting for transfers between devices, shifted(): return lax.ppermute(block, axis, route)  67.6 us
    psum x1, waiting for transfers between devices, spread(): return lax.psum(jnp.where(mine, array, jnp.zeros_like(array)), axis)  66.3 us
    all_gather x1, waiting for transfers between devices, per_device(): lax.all_gather(normed, 'seq', axis=0, tiled=True)  36.2 us
    squeeze x32, local copies, waits for them, and re-layouts, piece_scan(): lax.scan(advance, start, (to_blocks(rates), to_blocks(values), to_blocks(...  26.9 us
    dynamic_update_slice x32, local copies, waits for them, and re-layouts, piece_scan(): lax.scan(advance, start, (to_blocks(rates), to_blocks(values), to_blocks(...  21.4 us
  transfers between devices with their start and end apart: 30, of which 25 were waited for; matrix products, arithmetic and copies ran while one was open for 22% of the time, Pallas kernels for 0%

profile of v1, /device:TPU:0, one launch (start us, length us, event | category | flops | bytes accessed | tf_op | source)
XLA Modules:
  0.0 693.2 jit_solution(18442348756006711923)
XLA Ops:
  10.1 2.0 fusion.42
  12.2 7.0 %collective-permute-done.1 = bf16[2,256,256]{2,1,0:T(8,128)(2,1)S(1)} collective-permute-done((bf16[2,256,256]{2,1,0:T(8,128)(2,1)S(1)}, bf16[2,256,256]{2,1,0:T(8,128)(2,1)S(1)}, u32[]{:S(2)}, u32[]{:S(2)}) %collective-permute-start.1) | collective-permute-done | bytes 262176 | tf_op jit(solution)/shard_map/ppermute | solution.py:107
  19.2 3.0 collective-permute-start.5
  22.2 4.1 collective-permute-done.2
  26.2 3.0 collective-permute-start.6
  29.2 4.0 collective-permute-done.3
  33.3 3.0 collective-permute-start.7
  36.3 4.0 collective-permute-done.4
  46.0 2.3 gather_fusion
  49.6 36.2 %all-gather.4.cloned.1.call-done = bf16[2048,2048]{1,0:T(8,128)(2,1)} async-done(((bf16[128,2048]{1,0:T(8,128)(2,1)}), bf16[2048,2048]{1,0:T(8,128)(2,1)}) %all-gather.4.cloned.1.call-update) | async-done | bytes 8388624 | tf_op jit(solution)/shard_map/all_gather | solution.py:116
  85.7 7.2 %fusion.33 = f32[2048,512]{1,0:T(8,128)S(1)} fusion(bf16[2048,2048]{1,0:T(8,128)(2,1)} %all-gather.4.cloned.1.call-done, bf16[2048,256]{1,0:T(8,128)(2,1)} %bitcast.374, bf16[2048,256]{1,0:T(8,128)(2,1)S(1)} %bitcast.373), kind=kOutput, calls=%fused_computation.93 | convolution fusion | flops 4299161600 | bytes 14680064 | tf_op jit(solution)/shard_map/dot_general | solution.py:115
  94.9 2.3 multiply_convert_fusion
  97.2 2.8 fusion.59
  100.1 5.4 all-to-all-start.1
  106.8 88.7 %all-reduce.4.cloned.1.call-done = f32[2048,160]{0,1:T(8,128)} async-done(((f32[2048,160]{0,1:T(8,128)}), f32[2048,160]{0,1:T(8,128)}) %all-reduce.4.cloned.1.call-update) | async-done | bytes 1310736 | tf_op jit(solution)/shard_map/psum | solution.py:130
  195.5 2.7 fusion.32
  199.5 5.1 all-to-all-start
  206.1 2.6 copy.45
  208.6 2.8 reshape.1048
  213.0 7.5 %all-to-all-done = bf16[16,128,256]{1,2,0:T(8,128)(2,1)S(1)} async-done(((bf16[16,128,256]{1,2,0:T(8,128)(2,1)}), bf16[16,128,256]{1,2,0:T(8,128)(2,1)S(1)}, u32[]{:S(2)}, u32[]{:S(2)}) %all-to-all-start) | async-done | bytes 1048608 | tf_op jit(solution)/shard_map/all_to_all | solution.py:142
  223.8 2.2 copy.44
  230.3 65.8 %while.35 = (s32[]{:T(128)}, f32[1,16,4096]{2,1,0:T(8,128)S(1)}, f32[16,1,8,4096]{3,2,1,0:T(8,128)}, f32[16,1,8,4096]{3,2,1,0:T(8,128)}, f32[16,4096]{1,0:T(8,12...) while((s32[]{:T(128)}, f32[1,16,4096]{2,1,0:T(8,128)S(1)}, ...), condition=%wide.region_11.12_spmd.clone, body=%wide.region_2.11_spmd.clone.sunk | while | flops 4849667 | bytes 4347896 | solution.py:57
  296.1 148.6 %while.33 = (s32[]{:T(128)}, f32[16,4096]{1,0:T(8,128)S(1)}, f32[1,16,4096]{2,1,0:T(8,128)S(1)}, f32[1,16,4096]{2,1,0:T(8,128)S(1)}, s32[]{:T(128)}) while((s32[]{:T(128)}, f32[16,4096]{1,0:T(8,128)S(1)}, f32[1,16,4096]{2,1,0:T(8,128)S(1)}, f32[1,16,4096]{2,1,0:T(8,128)S(1)}, s32[]{:T(128)}) %tuple.124), condition=%wide.region_13.14_spmd, body=%wide.region_12.13_spmd.sunk | while | flops 131074 | bytes 2097253 | solution.py:158
  296.2 2.5 collective-permute-start
  298.7 3.9 collective-permute-done
  302.6 4.4 collective-permute-start
  307.0 4.9 collective-permute-done
  312.0 4.4 collective-permute-start
  316.4 6.1 collective-permute-done
  322.5 4.4 collective-permute-start
  326.9 6.1 collective-permute-done
  333.0 4.4 collective-permute-start
  337.5 5.2 collective-permute-done
  342.7 4.4 collective-permute-start
  347.1 4.4 collective-permute-done
  351.6 4.4 collective-permute-start
  356.0 3.9 collective-permute-done
  359.9 6.9 collective-permute-start
  366.8 5.6 collective-permute-done
  372.4 6.2 collective-permute-start
  378.6 4.4 collective-permute-done
  383.1 5.6 collective-permute-start
  388.8 3.9 collective-permute-done
  392.7 6.5 collective-permute-start
  399.2 3.9 collective-permute-done
  403.1 6.5 collective-permute-start
  409.6 3.9 collective-permute-done
  413.5 6.5 collective-permute-start
  420.0 3.9 collective-permute-done
  423.9 6.5 collective-permute-start
  430.4 3.9 collective-permute-done
  434.3 6.5 collective-permute-start
  440.9 3.9 collective-permute-done
  446.3 35.9 %while.34 = (s32[]{:T(128)}, f32[16,1,8,4096]{3,2,1,0:T(8,128)}, f32[16,1,8,16]{3,2,1,0:T(8,128)S(1)}, f32[16,1,8,4096]{3,2,1,0:T(8,128)}, f32[16,4096]{1,0:T(8,128)S(1)}, /*index=5*/f32[16,4096]{1,0:T(8,128)S(1)}, s32[]{:T(128)}) while((s32[]{:T(128)}, f32[16,1,8,4096]{3,2,1,0:T(8,128)}, f32[16,1,8,16]{3,2,1,0:T(8,128)S(1)}, ...), condition=%wide.region_16.17_spmd, body=%wide.region_14.16_spmd.sunk | while | flops 2064386 | bytes 1312853 | solution.py:71
  482.2 2.5 add.160
  485.4 2.3 fusion.30
  487.7 18.2 %all-to-all-start.2 = ((bf16[128,16,256]{2,0,1:T(8,128)(2,1)}), bf16[128,16,256]{2,0,1:T(8,128)(2,1)S(1)}, u32[]{:S(2)}, u32[]{:S(2)}) async-start(bf16[128,16,256]{2,0,1:T(8,128)(2,1)} %fusion.30), calls=%async_computation.2 | async-start | bytes 2097152 | tf_op jit(solution)/shard_map/all_to_all | solution.py:165
  507.0 12.2 %all-to-all-done.2 = bf16[128,16,256]{2,0,1:T(8,128)(2,1)S(1)} async-done(((bf16[128,16,256]{2,0,1:T(8,128)(2,1)}), bf16[128,16,256]{2,0,1:T(8,128)(2,1)S(1)}, u32[]{:S(2)}, u32[]{:S(2)}) %all-to-all-start.2) | async-done | bytes 1048608 | tf_op jit(solution)/shard_map/all_to_all | solution.py:165
  519.2 2.3 fusion.39
  521.6 6.8 convolution_convert_fusion
  529.0 66.3 %all-reduce.6.cloned.1.call-done = bf16[16,4096]{1,0:T(8,128)(2,1)} async-done(((bf16[16,4096]{1,0:T(8,128)(2,1)}), bf16[16,4096]{1,0:T(8,128)(2,1)}) %all-reduce.6.cloned.1.call-update) | async-done | bytes 131088 | tf_op jit(solution)/shard_map/psum | solution.py:24
  596.1 13.0 %all-gather = f32[128,256]{1,0:T(8,128)S(1)} all-gather(f32[16,256]{1,0:T(8,128)S(1)} %dynamic-slice_convert_fusion), channel_id=2, replica_groups=mesh['req'=8,'seq'=16] {'req'}, dimensions={0}, use_global_device_ids=true | all-gather | bytes 147456 | tf_op jit(solution)/shard_map/all_gather | solution.py:175
  609.8 74.3 %reduce-scatter.2.cloned.1.call-done = bf16[128,2048]{1,0:T(8,128)(2,1)} async-done(((bf16[2048,2048]{1,0:T(8,128)(2,1)}), bf16[128,2048]{1,0:T(8,128)(2,1)}) %reduce-scatter.2.cloned.1.call-update) | async-done | bytes 524304 | tf_op jit(solution)/shard_map/reduce_scatter | solution.py:169
  684.1 2.0 fusion.44
  (348 shorter events, 130.9 us)
Async XLA Ops:
  8.0 89.2 %copy-start = (bf16[256,160]{0,1:T(8,128)(2,1)S(1)}, bf16[256,160]{0,1:T(8,128)(2,1)}, u32[]{:S(2)}) copy-start(bf16[256,160]{0,1:T(8,128)(2,1)} %param.26) | copy-start | bytes 245764
  8.0 4.2 copy-start.6
  8.0 25.2 %copy-start.13 = (bf16[256]{0:T(256)(128)(2,1)S(1)}, bf16[256]{0:T(256)(128)(2,1)}, u32[]{:S(2)}) copy-start(bf16[256]{0:T(256)(128)(2,1)} %param.25) | copy-start | bytes 1540
  8.0 25.2 %copy-start.11 = (bf16[4,256]{1,0:T(4,128)(2,1)S(1)}, bf16[4,256]{1,0:T(4,128)(2,1)}, u32[]{:S(2)}) copy-start(bf16[4,256]{1,0:T(4,128)(2,1)} %param.24) | copy-start | bytes 6148
  8.0 77.7 %all-gather.4.cloned.1.call-start = ((), (), s32[]{:S(2)}) async-start(), calls=%async_computation.4 | async-start | bytes 8912896 | tf_op jit(solution)/shard_map/all_gather | solution.py:116
  12.1 183.3 %all-reduce.4.cloned.1.call-start = ((), (), s32[]{:S(2)}) async-start(), calls=%async_computation.5 | async-start | bytes 2621440 | tf_op jit(solution)/shard_map/psum | solution.py:130
  12.2 7.0 %collective-permute-start.1 = (bf16[2,256,256]{2,1,0:T(8,128)(2,1)S(1)}, bf16[2,256,256]{2,1,0:T(8,128)(2,1)S(1)}, u32[]{:S(2)}, u32[]{:S(2)}) collective-permute-start(bf16[2,256,256]{2,1,0:T(8,128)(2,1)S(1)} %copy-done.6), channel_id=1, source_target_pairs={{0,16},{16,32},{32,48},{48,64},{64,80},{80,96},{96,112},{112,0},{1... | collective-permute-start | bytes 786440 | tf_op jit(solution)/shard_map/ppermute | solution.py:107
  19.2 7.0 %collective-permute-start.2 = (bf16[2,256,256]{2,1,0:T(8,128)(2,1)S(1)}, bf16[2,256,256]{2,1,0:T(8,128)(2,1)S(1)}, u32[]{:S(2)}, u32[]{:S(2)}) collective-permute-start(bf16[2,256,256]{2,1,0:T(8,128)(2,1)S(1)} %collective-permute-done.1), channel_id=1, source_target_pairs={{0,16},{16,32},{32,48},{48,64},{64,80},{80,96},{96,112},{112,0},{1... | collective-permute-start | bytes 786440 | tf_op jit(solution)/shard_map/ppermute | solution.py:107
  19.2 7.0 %collective-permute-start.5 = (bf16[2,256,256]{2,1,0:T(8,128)(2,1)S(1)}, bf16[2,256,256]{2,1,0:T(8,128)(2,1)S(1)}, u32[]{:S(2)}, u32[]{:S(2)}) collective-permute-start(bf16[2,256,256]{2,1,0:T(8,128)(2,1)S(1)} %copy-done.6), channel_id=1, source_target_pairs={{16,0},{32,16},{48,32},{64,48},{80,64},{96,80},{112,96},{0,112},{1... | collective-permute-start | bytes 786440 | tf_op jit(solution)/shard_map/ppermute | solution.py:109
  26.2 7.0 %collective-permute-start.3 = (bf16[2,256,256]{2,1,0:T(8,128)(2,1)S(1)}, bf16[2,256,256]{2,1,0:T(8,128)(2,1)S(1)}, u32[]{:S(2)}, u32[]{:S(2)}) collective-permute-start(bf16[2,256,256]{2,1,0:T(8,128)(2,1)S(1)} %collective-permute-done.2), channel_id=1, source_target_pairs={{0,16},{16,32},{32,48},{48,64},{64,80},{80,96},{96,112},{112,0},{1... | collective-permute-start | bytes 786440 | tf_op jit(solution)/shard_map/ppermute | solution.py:107
  26.2 7.0 %collective-permute-start.6 = (bf16[2,256,256]{2,1,0:T(8,128)(2,1)S(1)}, bf16[2,256,256]{2,1,0:T(8,128)(2,1)S(1)}, u32[]{:S(2)}, u32[]{:S(2)}) collective-permute-start(bf16[2,256,256]{2,1,0:T(8,128)(2,1)S(1)} %collective-permute-done.5), channel_id=1, source_target_pairs={{16,0},{32,16},{48,32},{64,48},{80,64},{96,80},{112,96},{0,112},{1... | collective-permute-start | bytes 786440 | tf_op jit(solution)/shard_map/ppermute | solution.py:109
  33.2 7.0 %collective-permute-start.4 = (bf16[2,256,256]{2,1,0:T(8,128)(2,1)S(1)}, bf16[2,256,256]{2,1,0:T(8,128)(2,1)S(1)}, u32[]{:S(2)}, u32[]{:S(2)}) collective-permute-start(bf16[2,256,256]{2,1,0:T(8,128)(2,1)S(1)} %collective-permute-done.3), channel_id=1, source_target_pairs={{0,16},{16,32},{32,48},{48,64},{64,80},{80,96},{96,112},{112,0},{1... | collective-permute-start | bytes 786440 | tf_op jit(solution)/shard_map/ppermute | solution.py:107
  33.3 12.0 %collective-permute-start.7 = (bf16[2,256,256]{2,1,0:T(8,128)(2,1)S(1)}, bf16[2,256,256]{2,1,0:T(8,128)(2,1)S(1)}, u32[]{:S(2)}, u32[]{:S(2)}) collective-permute-start(bf16[2,256,256]{2,1,0:T(8,128)(2,1)S(1)} %collective-permute-done.6), channel_id=1, source_target_pairs={{16,0},{32,16},{48,32},{64,48},{80,64},{96,80},{112,96},{0,112},{1... | collective-permute-start | bytes 786440 | tf_op jit(solution)/shard_map/ppermute | solution.py:109
  92.9 1.9 copy-start.4
  100.0 5.5 copy-start.14
  100.0 5.5 copy-start.15
  100.0 95.4 %copy-start.12 = (bf16[128,256]{1,0:T(8,128)(2,1)S(1)}, bf16[128,256]{1,0:T(8,128)(2,1)}, u32[]{:S(2)}) copy-start(bf16[128,256]{1,0:T(8,128)(2,1)} %param.27) | copy-start | bytes 196612
  100.1 99.5 %all-to-all-start.1 = ((bf16[16,128,256]{2,1,0:T(8,128)(2,1)}), bf16[16,128,256]{2,1,0:T(8,128)(2,1)S(1)}, u32[]{:S(2)}, u32[]{:S(2)}) async-start(bf16[16,128,256]{2,1,0:T(8,128)(2,1)} %bitcast.27), calls=%async_computation.1 | async-start | bytes 2097152 | tf_op jit(solution)/shard_map/all_to_all | solution.py:141
  198.2 7.0 %copy-start.10 = (f32[4096]{0:T(1024)S(1)}, f32[4096]{0:T(1024)}, u32[]{:S(2)}) copy-start(f32[4096]{0:T(1024)} %param.30) | copy-start | bytes 49156
  199.5 20.9 %all-to-all-start = ((bf16[16,128,256]{1,2,0:T(8,128)(2,1)}), bf16[16,128,256]{1,2,0:T(8,128)(2,1)S(1)}, u32[]{:S(2)}, u32[]{:S(2)}) async-start(bf16[16,128,256]{1,2,0:T(8,128)(2,1)} %copy.43), calls=%async_computation | async-start | bytes 2097152 | tf_op jit(solution)/shard_map/all_to_all | solution.py:142
  204.6 316.9 %all-gather.6.cloned.1.call-start = ((), (), s32[]{:S(2)}) async-start(), calls=%async_computation.6 | async-start | bytes 1179648 | tf_op jit(solution)/shard_map/all_gather | solution.py:140
  220.9 1.4 copy-start.3
  222.2 5.5 copy-start.7
  296.2 6.3 collective-permute-start
  302.6 9.4 %collective-permute-start = (f32[16,4096]{1,0:T(8,128)S(1)}, f32[16,4096]{1,0:T(8,128)S(1)}, u32[]{:S(2)}, u32[]{:S(2)}) collective-permute-start(f32[16,4096]{1,0:T(8,128)S(1)} %bitcast_add_fusion.3), channel_id=1, source_target_pairs={{0,1},{1,2},{2,3},{3,4},{4,5},{5,6},{6,7},{7,8},{8,9},{9,10},{10,1... | collective-permute-start | bytes 786440 | tf_op jit(solution)/shard_map/while/body/eval_jaxpr/ppermute | solution.py:19
  312.0 10.5 %collective-permute-start = (f32[16,4096]{1,0:T(8,128)S(1)}, f32[16,4096]{1,0:T(8,128)S(1)}, u32[]{:S(2)}, u32[]{:S(2)}) collective-permute-start(f32[16,4096]{1,0:T(8,128)S(1)} %bitcast_add_fusion.3), channel_id=1, source_target_pairs={{0,1},{1,2},{2,3},{3,4},{4,5},{5,6},{6,7},{7,8},{8,9},{9,10},{10,1... | collective-permute-start | bytes 786440 | tf_op jit(solution)/shard_map/while/body/eval_jaxpr/ppermute | solution.py:19
  322.5 10.5 %collective-permute-start = (f32[16,4096]{1,0:T(8,128)S(1)}, f32[16,4096]{1,0:T(8,128)S(1)}, u32[]{:S(2)}, u32[]{:S(2)}) collective-permute-start(f32[16,4096]{1,0:T(8,128)S(1)} %bitcast_add_fusion.3), channel_id=1, source_target_pairs={{0,1},{1,2},{2,3},{3,4},{4,5},{5,6},{6,7},{7,8},{8,9},{9,10},{10,1... | collective-permute-start | bytes 786440 | tf_op jit(solution)/shard_map/while/body/eval_jaxpr/ppermute | solution.py:19
  333.0 9.6 %collective-permute-start = (f32[16,4096]{1,0:T(8,128)S(1)}, f32[16,4096]{1,0:T(8,128)S(1)}, u32[]{:S(2)}, u32[]{:S(2)}) collective-permute-start(f32[16,4096]{1,0:T(8,128)S(1)} %bitcast_add_fusion.3), channel_id=1, source_target_pairs={{0,1},{1,2},{2,3},{3,4},{4,5},{5,6},{6,7},{7,8},{8,9},{9,10},{10,1... | collective-permute-start | bytes 786440 | tf_op jit(solution)/shard_map/while/body/eval_jaxpr/ppermute | solution.py:19
  342.7 8.8 %collective-permute-start = (f32[16,4096]{1,0:T(8,128)S(1)}, f32[16,4096]{1,0:T(8,128)S(1)}, u32[]{:S(2)}, u32[]{:S(2)}) collective-permute-start(f32[16,4096]{1,0:T(8,128)S(1)} %bitcast_add_fusion.3), channel_id=1, source_target_pairs={{0,1},{1,2},{2,3},{3,4},{4,5},{5,6},{6,7},{7,8},{8,9},{9,10},{10,1... | collective-permute-start | bytes 786440 | tf_op jit(solution)/shard_map/while/body/eval_jaxpr/ppermute | solution.py:19
  351.6 8.3 %collective-permute-start = (f32[16,4096]{1,0:T(8,128)S(1)}, f32[16,4096]{1,0:T(8,128)S(1)}, u32[]{:S(2)}, u32[]{:S(2)}) collective-permute-start(f32[16,4096]{1,0:T(8,128)S(1)} %bitcast_add_fusion.3), channel_id=1, source_target_pairs={{0,1},{1,2},{2,3},{3,4},{4,5},{5,6},{6,7},{7,8},{8,9},{9,10},{10,1... | collective-permute-start | bytes 786440 | tf_op jit(solution)/shard_map/while/body/eval_jaxpr/ppermute | solution.py:19
  359.9 12.5 %collective-permute-start = (f32[16,4096]{1,0:T(8,128)S(1)}, f32[16,4096]{1,0:T(8,128)S(1)}, u32[]{:S(2)}, u32[]{:S(2)}) collective-permute-start(f32[16,4096]{1,0:T(8,128)S(1)} %bitcast_add_fusion.3), channel_id=1, source_target_pairs={{0,1},{1,2},{2,3},{3,4},{4,5},{5,6},{6,7},{7,8},{8,9},{9,10},{10,1... | collective-permute-start | bytes 786440 | tf_op jit(solution)/shard_map/while/body/eval_jaxpr/ppermute | solution.py:19
  372.4 10.7 %collective-permute-start = (f32[16,4096]{1,0:T(8,128)S(1)}, f32[16,4096]{1,0:T(8,128)S(1)}, u32[]{:S(2)}, u32[]{:S(2)}) collective-permute-start(f32[16,4096]{1,0:T(8,128)S(1)} %bitcast_add_fusion.3), channel_id=1, source_target_pairs={{0,1},{1,2},{2,3},{3,4},{4,5},{5,6},{6,7},{7,8},{8,9},{9,10},{10,1... | collective-permute-start | bytes 786440 | tf_op jit(solution)/shard_map/while/body/eval_jaxpr/ppermute | solution.py:19
  383.1 9.5 %collective-permute-start = (f32[16,4096]{1,0:T(8,128)S(1)}, f32[16,4096]{1,0:T(8,128)S(1)}, u32[]{:S(2)}, u32[]{:S(2)}) collective-permute-start(f32[16,4096]{1,0:T(8,128)S(1)} %bitcast_add_fusion.3), channel_id=1, source_target_pairs={{0,1},{1,2},{2,3},{3,4},{4,5},{5,6},{6,7},{7,8},{8,9},{9,10},{10,1... | collective-permute-start | bytes 786440 | tf_op jit(solution)/shard_map/while/body/eval_jaxpr/ppermute | solution.py:19
  392.7 10.4 %collective-permute-start = (f32[16,4096]{1,0:T(8,128)S(1)}, f32[16,4096]{1,0:T(8,128)S(1)}, u32[]{:S(2)}, u32[]{:S(2)}) collective-permute-start(f32[16,4096]{1,0:T(8,128)S(1)} %bitcast_add_fusion.3), channel_id=1, source_target_pairs={{0,1},{1,2},{2,3},{3,4},{4,5},{5,6},{6,7},{7,8},{8,9},{9,10},{10,1... | collective-permute-start | bytes 786440 | tf_op jit(solution)/shard_map/while/body/eval_jaxpr/ppermute | solution.py:19
  403.1 10.4 %collective-permute-start = (f32[16,4096]{1,0:T(8,128)S(1)}, f32[16,4096]{1,0:T(8,128)S(1)}, u32[]{:S(2)}, u32[]{:S(2)}) collective-permute-start(f32[16,4096]{1,0:T(8,128)S(1)} %bitcast_add_fusion.3), channel_id=1, source_target_pairs={{0,1},{1,2},{2,3},{3,4},{4,5},{5,6},{6,7},{7,8},{8,9},{9,10},{10,1... | collective-permute-start | bytes 786440 | tf_op jit(solution)/shard_map/while/body/eval_jaxpr/ppermute | solution.py:19
  413.5 10.4 %collective-permute-start = (f32[16,4096]{1,0:T(8,128)S(1)}, f32[16,4096]{1,0:T(8,128)S(1)}, u32[]{:S(2)}, u32[]{:S(2)}) collective-permute-start(f32[16,4096]{1,0:T(8,128)S(1)} %bitcast_add_fusion.3), channel_id=1, source_target_pairs={{0,1},{1,2},{2,3},{3,4},{4,5},{5,6},{6,7},{7,8},{8,9},{9,10},{10,1... | collective-permute-start | bytes 786440 | tf_op jit(solution)/shard_map/while/body/eval_jaxpr/ppermute | solution.py:19
  423.9 10.4 %collective-permute-start = (f32[16,4096]{1,0:T(8,128)S(1)}, f32[16,4096]{1,0:T(8,128)S(1)}, u32[]{:S(2)}, u32[]{:S(2)}) collective-permute-start(f32[16,4096]{1,0:T(8,128)S(1)} %bitcast_add_fusion.3), channel_id=1, source_target_pairs={{0,1},{1,2},{2,3},{3,4},{4,5},{5,6},{6,7},{7,8},{8,9},{9,10},{10,1... | collective-permute-start | bytes 786440 | tf_op jit(solution)/shard_map/while/body/eval_jaxpr/ppermute | solution.py:19
  434.3 10.4 %collective-permute-start = (f32[16,4096]{1,0:T(8,128)S(1)}, f32[16,4096]{1,0:T(8,128)S(1)}, u32[]{:S(2)}, u32[]{:S(2)}) collective-permute-start(f32[16,4096]{1,0:T(8,128)S(1)} %bitcast_add_fusion.3), channel_id=1, source_target_pairs={{0,1},{1,2},{2,3},{3,4},{4,5},{5,6},{6,7},{7,8},{8,9},{9,10},{10,1... | collective-permute-start | bytes 786440 | tf_op jit(solution)/shard_map/while/body/eval_jaxpr/ppermute | solution.py:19
  484.7 0.7 copy-start.9
  487.7 18.2 %copy-start.5 = (f32[16,4096]{1,0:T(8,128)S(1)}, f32[16,4096]{1,0:T(8,128)}, u32[]{:S(2)}) copy-start(f32[16,4096]{1,0:T(8,128)} %param.29) | copy-start | bytes 786436
  487.7 18.2 %copy-start.8 = (f32[1,1,4096]{2,1,0:T(1,128)S(1)}, f32[1,1,4096]{2,1,0:T(1,128)}, u32[]{:S(2)}) copy-start(f32[1,1,4096]{2,1,0:T(1,128)} %copy-done.7) | copy-start | bytes 49156
  487.7 31.5 %all-to-all-start.2 = ((bf16[128,16,256]{2,0,1:T(8,128)(2,1)}), bf16[128,16,256]{2,0,1:T(8,128)(2,1)S(1)}, u32[]{:S(2)}, u32[]{:S(2)}) async-start(bf16[128,16,256]{2,0,1:T(8,128)(2,1)} %fusion.30), calls=%async_computation.2 | async-start | bytes 2097152 | tf_op jit(solution)/shard_map/all_to_all | solution.py:165
  505.9 89.5 %all-reduce.6.cloned.1.call-start = ((), (), s32[]{:S(2)}) async-start(), calls=%async_computation.8 | async-start | bytes 262144 | tf_op jit(solution)/shard_map/psum | solution.py:24
  506.7 177.3 %reduce-scatter.2.cloned.1.call-start = ((), (), s32[]{:S(2)}) async-start(), calls=%async_computation.7 | async-start | bytes 8912896 | tf_op jit(solution)/shard_map/reduce_scatter | solution.py:169
  528.4 0.7 copy-start.16
  528.4 155.7 %copy-start.2 = (bf16[1,128,2048]{2,1,0:T(8,128)(2,1)S(1)}, bf16[1,128,2048]{2,1,0:T(8,128)(2,1)}, u32[]{:S(2)}) copy-start(bf16[1,128,2048]{2,1,0:T(8,128)(2,1)} %param.19) | copy-start | bytes 1572868
  528.4 157.6 %copy-start.1 = (bf16[256,160]{0,1:T(8,128)(2,1)S(1)}, bf16[256,160]{0,1:T(8,128)(2,1)}, u32[]{:S(2)}) copy-start(bf16[256,160]{0,1:T(8,128)(2,1)} %param.26) | copy-start | bytes 245764
Sparse Core Ops, SparseCore 0:
  12.3 73.4 all-gather.3
  100.2 95.2 all-reduce.3
  510.5 84.8 all-reduce.5
  598.6 85.3 reduce-scatter.1
Sparse Core Ops, SparseCore 1:
  206.8 24.6 all-gather.5
